TPU v7x, 128 devices: a whole 4x4x4 slice. The times are simulated.
128 devices in a mesh: dp: 16 (over x, y), feat: 8 (over z, core).
Axes of the slice: x: 4, y: 4, z: 4, core: 2. Of those that a mesh axis runs over, the one named last changes fastest.
Arguments:
- images: bfloat16 [8192, 3072], P(('dp', 'feat')), may hold values from -6 to 6
- labels: int32 [8192], P('dp'), may hold values from 0 to 999
- predictions: float32 [8192, 1000], P('dp'), may hold values from -2 to 2
- filters: bfloat16 [75, 1024], P(None, 'feat'), may hold values from -0.75 to 0.75
- biases: float32 [1024], P('feat'), may hold values from -3 to 3
Outputs:
- weights: float32 [4096, 1000], P('feat')
- new_residual: float32 [8192, 1000], P(('dp', 'feat'))
All inputs are finite; a program needn't handle non-finite values.
Results may differ from a plain program's by a relative error of at most 0.007.
The roundings to bfloat16 on the way count: a program that leaves them out, or rounds other values in their place, can miss the bound.
Values may be sent and summed in bfloat16 or wider, within the bound.
No kernel may reach another device: no remote copies, remote signals or barrier semaphores. Data moves between devices by JAX's collectives and lax.ppermute only.
A program may use at most 192 MiB of HBM per device.

v0:
```python
import math

import jax
import jax.numpy as jnp
from jax import lax
from jax.sharding import PartitionSpec as P

SIDE = 32
CHAN = 3
KSIZE = 5


def chol_solve(factor, rhs):
    middle = lax.linalg.triangular_solve(factor, rhs, left_side=True, lower=True, transpose_a=False)
    return lax.linalg.triangular_solve(factor, middle, left_side=True, lower=True, transpose_a=True)


def split_parts(values):
    upper = values.astype(jnp.bfloat16)
    lower = (values - upper.astype(jnp.float32)).astype(jnp.bfloat16)
    return (upper, lower)


def left_product(feats, other):
    return lax.dot_general(
        feats, other, (((0,), (0,)), ((), ())), preferred_element_type=jnp.float32
    )


def conv_pool(imgs, kernel, offsets):
    count = imgs.shape[0]
    filt_count = kernel.shape[3]
    pics = imgs.reshape(count, SIDE, SIDE, CHAN)
    response = lax.conv_general_dilated(
        pics,
        kernel,
        (1, 1),
        "VALID",
        dimension_numbers=("NHWC", "HWIO", "NHWC"),
        preferred_element_type=jnp.float32,
    )
    response = jnp.maximum(response + offsets, 0.0)
    half = (SIDE - KSIZE + 1) // 2
    pooled = response.reshape(count, 2, half, 2, half, filt_count).mean(axis=(2, 4))
    return jnp.transpose(pooled, (0, 3, 1, 2)).reshape(count, 4 * filt_count).astype(jnp.bfloat16)


def shards(images, labels, predictions, filters, biases):
    filt_count = filters.shape[1]
    kernel = filters.reshape(KSIZE, KSIZE, CHAN, filt_count)
    share = images.shape[0]
    total_images = share * lax.axis_size("feat") * lax.axis_size("dp")
    piece = lax.all_gather(images, "feat", axis=0, tiled=True)
    count = piece.shape[0]
    group = math.gcd(count, 128)
    blocks = piece.reshape(count // group, group, piece.shape[1])
    out = lax.map(lambda part: conv_pool(part, kernel, biases), blocks)
    feats = out.reshape(count, 4 * filt_count)
    width = feats.shape[1]
    residual = (
        labels[:, None] == jnp.arange(predictions.shape[1], dtype=jnp.int32)[None, :]
    ).astype(jnp.float32) - predictions
    res_upper, res_lower = split_parts(residual)
    gram = left_product(feats, feats)
    cross = left_product(feats, res_upper) + left_product(feats, res_lower)
    gram, cross = lax.psum((gram, cross), "dp")
    gram = gram / total_images + 0.5 * jnp.eye(width, dtype=jnp.float32)
    cross = cross / total_images
    factor = jnp.linalg.cholesky(gram)
    solved = chol_solve(factor, cross)
    sol_upper, sol_lower = split_parts(solved)
    fitted = lax.psum_scatter(
        (
            jnp.dot(feats, sol_upper, preferred_element_type=jnp.float32)
            + jnp.dot(feats, sol_lower, preferred_element_type=jnp.float32)
        ).astype(jnp.bfloat16),
        "feat",
        scatter_dimension=0,
        tiled=True,
    ).astype(jnp.float32)
    mine = lax.dynamic_slice_in_dim(residual, lax.axis_index("feat") * share, share, 0)
    return (solved, mine - fitted)


def solution(mesh):
    placed = (P(("dp", "feat"), None), P("dp"), P("dp", None), P(None, "feat"), P("feat"))
    return jax.shard_map(
        shards,
        mesh=mesh,
        in_specs=placed,
        out_specs=(P("feat", None), P(("dp", "feat"), None)),
        check_vma=False,
    )
```

profile of v0, /device:TPU:0, one launch (start us, length us, event | category | flops | bytes accessed | tf_op | source)
XLA Modules:
  0.0 508.4 jit_solution(16264020575135141605)
XLA Ops:
  12.2 27.9 %all-gather.2.cloned.1.call-done = bf16[512,3072]{1,0:T(8,128)(2,1)} async-done(((bf16[64,3072]{1,0:T(8,128)(2,1)}), bf16[512,3072]{1,0:T(8,128)(2,1)}) %all-gather.2.cloned.1.call-update) | async-done | bytes 3145744 | tf_op jit(solution)/shard_map/all_gather | solution.py:53
  40.1 152.3 %while.11 = (s32[]{:T(128)}, bf16[4,128,512]{1,2,0:T(8,128)(2,1)}, bf16[4,128,3072]{2,1,0:T(8,128)(2,1)}, bf16[5,5,3,128]{3,2,1,0:T(4,128)(2,1)S(1)}, f32[128]{0:T(128)S(1)}, /*index=5*/s32[]{:T(128)}, f32[]{:T(128)}) while((s32[]{:T(128)}, bf16[4,128,512]{1,2,0:T(8,128)(2,1)}, bf16[4,128,3072]{2,1,0:T(8,128)(2,1)}, ...), condition=%wide.region_2.3_spmd, body=%wide.region_0.2_spmd.sunk | while | flops 1965359104 | bytes 109465424 | solution.py:57
  42.1 19.1 %add_maximum_fusion.2 = f32[128,28,28,128]{3,0,2,1:T(8,128)} fusion(f32[128]{0:T(128)S(1)} %get-tuple-element.167, bf16[128,32,32,3]{0,3,2,1:T(4,128)(2,1)S(1)} %reshape.101, bf16[5,5,3,128]{3,2,1,0:T(4,128)(2,1)S(1)} %get-tuple-element.166), kind=kOutput, calls=%fused_computation.clone.1 | convolution fusion | flops 1952448512 | bytes 52186368 | tf_op jit(solution)/shard_map/while/body/eval_jaxpr/conv_general_dilated | solution.py:34
  61.2 16.1 %reduce_sum.10 = f32[128,2,2,128]{3,0,2,1:T(8,128)S(1)} reduce(f32[128,2,14,2,14,128]{5,0,4,3,2,1:T(8,128)} %bitcast.85, f32[]{:T(128)} %constant.173.clone.1..sunk), dimensions={2,4}, to_apply=%region_1.1 | reduce | flops 12779520 | bytes 51642372 | tf_op jit(solution)/shard_map/while/body/eval_jaxpr/reduce_sum | solution.py:44
  80.1 19.1 %add_maximum_fusion.2 = f32[128,28,28,128]{3,0,2,1:T(8,128)} fusion(f32[128]{0:T(128)S(1)} %get-tuple-element.167, bf16[128,32,32,3]{0,3,2,1:T(4,128)(2,1)S(1)} %reshape.101, bf16[5,5,3,128]{3,2,1,0:T(4,128)(2,1)S(1)} %get-tuple-element.166), kind=kOutput, calls=%fused_computation.clone.1 | convolution fusion | flops 1952448512 | bytes 52186368 | tf_op jit(solution)/shard_map/while/body/eval_jaxpr/conv_general_dilated | solution.py:34
  99.3 16.1 %reduce_sum.10 = f32[128,2,2,128]{3,0,2,1:T(8,128)S(1)} reduce(f32[128,2,14,2,14,128]{5,0,4,3,2,1:T(8,128)} %bitcast.85, f32[]{:T(128)} %constant.173.clone.1..sunk), dimensions={2,4}, to_apply=%region_1.1 | reduce | flops 12779520 | bytes 51642372 | tf_op jit(solution)/shard_map/while/body/eval_jaxpr/reduce_sum | solution.py:44
  118.2 19.1 %add_maximum_fusion.2 = f32[128,28,28,128]{3,0,2,1:T(8,128)} fusion(f32[128]{0:T(128)S(1)} %get-tuple-element.167, bf16[128,32,32,3]{0,3,2,1:T(4,128)(2,1)S(1)} %reshape.101, bf16[5,5,3,128]{3,2,1,0:T(4,128)(2,1)S(1)} %get-tuple-element.166), kind=kOutput, calls=%fused_computation.clone.1 | convolution fusion | flops 1952448512 | bytes 52186368 | tf_op jit(solution)/shard_map/while/body/eval_jaxpr/conv_general_dilated | solution.py:34
  137.3 16.1 %reduce_sum.10 = f32[128,2,2,128]{3,0,2,1:T(8,128)S(1)} reduce(f32[128,2,14,2,14,128]{5,0,4,3,2,1:T(8,128)} %bitcast.85, f32[]{:T(128)} %constant.173.clone.1..sunk), dimensions={2,4}, to_apply=%region_1.1 | reduce | flops 12779520 | bytes 51642372 | tf_op jit(solution)/shard_map/while/body/eval_jaxpr/reduce_sum | solution.py:44
  156.3 19.1 %add_maximum_fusion.2 = f32[128,28,28,128]{3,0,2,1:T(8,128)} fusion(f32[128]{0:T(128)S(1)} %get-tuple-element.167, bf16[128,32,32,3]{0,3,2,1:T(4,128)(2,1)S(1)} %reshape.101, bf16[5,5,3,128]{3,2,1,0:T(4,128)(2,1)S(1)} %get-tuple-element.166), kind=kOutput, calls=%fused_computation.clone.1 | convolution fusion | flops 1952448512 | bytes 52186368 | tf_op jit(solution)/shard_map/while/body/eval_jaxpr/conv_general_dilated | solution.py:34
  175.4 16.1 %reduce_sum.10 = f32[128,2,2,128]{3,0,2,1:T(8,128)S(1)} reduce(f32[128,2,14,2,14,128]{5,0,4,3,2,1:T(8,128)} %bitcast.85, f32[]{:T(128)} %constant.173.clone.1..sunk), dimensions={2,4}, to_apply=%region_1.1 | reduce | flops 12779520 | bytes 51642372 | tf_op jit(solution)/shard_map/while/body/eval_jaxpr/reduce_sum | solution.py:44
  193.8 2.7 convolution_bitcast_fusion
  199.5 95.2 %all-reduce.4.cloned.1.call-done = (f32[512,1000]{0,1:T(8,128)}, f32[512,512]{1,0:T(8,128)}) async-done(((f32[512,1000]{0,1:T(8,128)}, f32[512,512]{1,0:T(8,128)}), (f32[512,1000]{0,1:T(8,128)}, f32[512,512]{1,0:T(8,128)})) %all-reduce.4.cloned.1.call-update) | async-done | bytes 3096592 | tf_op jit(solution)/shard_map/psum | solution.py:66
  297.1 2.5 copy.22
  302.4 11.7 %cholesky.103 = f32[128,128]{1,0:T(8,128)S(1)} custom-call(f32[128,128]{1,0:T(8,128)S(1)} %cholesky.263), custom_call_target="Cholesky" | custom-call | tf_op jit(solution)/shard_map/jit(cholesky)/cholesky | solution.py:69
  315.2 9.8 %custom-call.32 = f32[1,128,128]{1,2,0:T(8,128)S(1)} custom-call(f32[1,128,128]{2,1,0:T(8,128)S(1)} %get-tuple-element.84), custom_call_target="InvertDiagBlocksLowerTriangular" | custom-call | tf_op jit(solution)/shard_map/jit(cholesky)/cholesky | solution.py:69
  328.2 11.7 %cholesky.215 = f32[128,128]{1,0:T(8,128)S(1)} custom-call(f32[128,128]{1,0:T(8,128)S(1)} %cholesky.267), custom_call_target="Cholesky" | custom-call | tf_op jit(solution)/shard_map/jit(cholesky)/cholesky | solution.py:69
  340.6 10.2 %custom-call.33 = f32[1,128,128]{1,2,0:T(8,128)S(1)} custom-call(f32[1,128,128]{2,1,0:T(8,128)S(1)} %get-tuple-element.81), custom_call_target="InvertDiagBlocksLowerTriangular" | custom-call | tf_op jit(solution)/shard_map/jit(cholesky)/cholesky | solution.py:69
  353.1 11.7 %cholesky.236 = f32[128,128]{1,0:T(8,128)S(1)} custom-call(f32[128,128]{1,0:T(8,128)S(1)} %cholesky.272), custom_call_target="Cholesky" | custom-call | tf_op jit(solution)/shard_map/jit(cholesky)/cholesky | solution.py:69
  366.2 9.8 %custom-call.34 = f32[1,128,128]{1,2,0:T(8,128)S(1)} custom-call(f32[1,128,128]{2,1,0:T(8,128)S(1)} %get-tuple-element.78), custom_call_target="InvertDiagBlocksLowerTriangular" | custom-call | tf_op jit(solution)/shard_map/jit(cholesky)/cholesky | solution.py:69
  378.3 11.7 %cholesky.253 = f32[128,128]{1,0:T(8,128)S(1)} custom-call(f32[128,128]{1,0:T(8,128)S(1)} %convolution_subtract_fusion.6), custom_call_target="Cholesky" | custom-call | tf_op jit(solution)/shard_map/jit(cholesky)/cholesky | solution.py:69
  394.6 2.3 select_select_fusion
  396.9 11.6 %while.12 = (s32[]{:T(128)}, f32[512,512]{1,0:T(8,128)}, s32[4,2]{0,1:T(2,128)S(1)}, f32[4,128,128]{2,1,0:T(8,128)S(1)}, s32[]{:T(128)}) while((s32[]{:T(128)}, f32[512,512]{1,0:T(8,128)}, s32[4,2]{0,1:T(2,128)S(1)}, f32[4,128,128]{2,1,0:T(8,128)S(1)}, s32[]{:T(128)}) %tuple.50), condition=%wide.while_cond, body=%wide.while_body.sunk | while | flops 2 | bytes 131181 | solution.py:15
  408.5 39.3 %custom-call.35 = f32[4,128,128]{1,2,0:T(8,128)S(1)} custom-call(f32[4,128,128]{2,1,0:T(8,128)S(1)} %get-tuple-element.37), custom_call_target="InvertDiagBlocksLowerTriangular" | custom-call | tf_op jit(solution)/shard_map/triangular_solve | solution.py:15
  468.4 31.6 %reduce-scatter.2.cloned.1.call-done = bf16[64,1000]{1,0:T(8,128)(2,1)} async-done(((bf16[512,1000]{1,0:T(8,128)(2,1)}), bf16[64,1000]{1,0:T(8,128)(2,1)}) %reduce-scatter.2.cloned.1.call-update) | async-done | bytes 128016 | tf_op jit(solution)/shard_map/reduce_scatter | solution.py:72
  (102 shorter events, 72.1 us)
Async XLA Ops:
  7.2 32.9 %all-gather.2.cloned.1.call-start = ((), (), s32[]{:S(2)}) async-start(), calls=%async_computation.1 | async-start | bytes 3538944 | tf_op jit(solution)/shard_map/all_gather | solution.py:53
  7.9 286.8 %all-reduce.4.cloned.1.call-start = ((), (), s32[]{:S(2)}) async-start(), calls=%async_computation.3 | async-start | bytes 6193152 | tf_op jit(solution)/shard_map/psum | solution.py:66
  8.7 1.9 copy-start.4
  10.7 29.4 %copy-start.5 = (f32[128]{0:T(128)S(1)}, f32[128]{0:T(128)}, u32[]{:S(2)}) copy-start(f32[128]{0:T(128)} %param.11) | copy-start | bytes 1540
  192.4 4.1 copy-start
  199.2 300.8 %reduce-scatter.2.cloned.1.call-start = ((), (), s32[]{:S(2)}) async-start(), calls=%async_computation.2 | async-start | bytes 1179648 | tf_op jit(solution)/shard_map/reduce_scatter | solution.py:72
  301.4 1.0 copy-start.3
  447.8 2.9 copy-start.2
  465.3 1.3 copy-start.1
Sparse Core Ops, SparseCore 0:
  9.7 30.3 all-gather.1
  199.4 95.3 all-reduce.3
  468.5 31.4 reduce-scatter.1
where the time goes:
time: 514 us; the launch traced here: 508 us
  other arithmetic  196 us (38%)
  waiting for transfers between devices  155 us (30%)
  matrix products  108 us (21%)
  local copies, waits for them, and re-layouts  31.8 us (6%)
  between operations  16.9 us (3%)
    psum x1, waiting for transfers between devices, shards(): gram, cross = lax.psum((gram, cross), 'dp')  95.2 us
    another operation x14, other arithmetic, shards(): factor = jnp.linalg.cholesky(gram)  80.6 us
    conv_general_dilated x4, matrix products, conv_pool(): lax.conv_general_dilated(pics, kernel, (1, 1), 'VALID', dimension_numbers...  76.5 us
    reduce_sum x4, other arithmetic, conv_pool(): response.reshape(count, 2, half, 2, half, filt_count).mean(axis=(2, 4))  64.5 us
    another operation x4, other arithmetic, chol_solve(): lax.linalg.triangular_solve(factor, middle, left_side=True, lower=True, t...  41.8 us
    reduce_scatter x1, waiting for transfers between devices, shards(): lax.psum_scatter((jnp.dot(feats, sol_upper, preferred_element_type=jnp.fl...  31.6 us
    all_gather x1, waiting for transfers between devices, shards(): piece = lax.all_gather(images, 'feat', axis=0, tiled=True)  27.9 us
    another operation x12, local copies, waits for them, and re-layouts  11.5 us
  transfers between devices with their start and end apart: 3, of which 3 were waited for; matrix products, arithmetic and copies ran while one was open for 1% of the time, Pallas kernels for 0%

commit v1 on v0

--- a/solution.py
+++ b/solution.py
@@ -61,9 +61,10 @@
         labels[:, None] == jnp.arange(predictions.shape[1], dtype=jnp.int32)[None, :]
     ).astype(jnp.float32) - predictions
     res_upper, res_lower = split_parts(residual)
-    gram = left_product(feats, feats)
+    gram = lax.psum(left_product(feats, feats), "dp")
     cross = left_product(feats, res_upper) + left_product(feats, res_lower)
-    gram, cross = lax.psum((gram, cross), "dp")
+    cross, gram = lax.optimization_barrier((cross, gram))
+    cross = lax.psum(cross, "dp")
     gram = gram / total_images + 0.5 * jnp.eye(width, dtype=jnp.float32)
     cross = cross / total_images
     factor = jnp.linalg.cholesky(gram)

time: 514 us -> 533 us (1.037)
  waiting for transfers between devices: 155 us -> 171 us
    psum x1 -> x2, waiting for transfers between devices: 95.2 us -> 110 us  [the longest x1 82 us: shards(): gram = lax.psum(left_product(feats, feats), 'dp')]
  transfers between devices with their start and end apart: 3 -> 4, of which waited for: 3 -> 4; matrix products, arithmetic and copies ran while one was open for 1% -> 13% of each run, Pallas kernels for 0% -> 0%
where the time goes in v1:
time: 533 us; the launch traced here: 528 us
  other arithmetic  198 us (37%)
  waiting for transfers between devices  171 us (32%)
  matrix products  108 us (20%)
  local copies, waits for them, and re-layouts  34.7 us (7%)
  between operations  16.6 us (3%)
    psum x1, waiting for transfers between devices, shards(): gram = lax.psum(left_product(feats, feats), 'dp')  82 us
    another operation x14, other arithmetic, shards(): factor = jnp.linalg.cholesky(gram)  80.7 us
    conv_general_dilated x4, matrix products, conv_pool(): lax.conv_general_dilated(pics, kernel, (1, 1), 'VALID', dimension_numbers...  76.5 us
    reduce_sum x4, other arithmetic, conv_pool(): response.reshape(count, 2, half, 2, half, filt_count).mean(axis=(2, 4))  64.5 us
    another operation x4, other arithmetic, chol_solve(): lax.linalg.triangular_solve(factor, middle, left_side=True, lower=True, t...  43.1 us
    reduce_scatter x1, waiting for transfers between devices, shards(): lax.psum_scatter((jnp.dot(feats, sol_upper, preferred_element_type=jnp.fl...  31.7 us
    psum x1, waiting for transfers between devices, shards(): cross = lax.psum(cross, 'dp')  28.5 us
    all_gather x1, waiting for transfers between devices, shards(): piece = lax.all_gather(images, 'feat', axis=0, tiled=True)  28 us
  transfers between devices with their start and end apart: 4, of which 4 were waited for; matrix products, arithmetic and copies ran while one was open for 13% of the time, Pallas kernels for 0%

profile of v1, /device:TPU:0, one launch (start us, length us, event | category | flops | bytes accessed | tf_op | source)
XLA Modules:
  0.0 528.2 jit_solution(10686514619989856401)
XLA Ops:
  12.1 28.0 %all-gather.2.cloned.1.call-done = bf16[512,3072]{1,0:T(8,128)(2,1)} async-done(((bf16[64,3072]{1,0:T(8,128)(2,1)}), bf16[512,3072]{1,0:T(8,128)(2,1)}) %all-gather.2.cloned.1.call-update) | async-done | bytes 3145744 | tf_op jit(solution)/shard_map/all_gather | solution.py:53
  40.1 152.3 %while.11 = (s32[]{:T(128)}, bf16[4,128,512]{1,2,0:T(8,128)(2,1)}, bf16[4,128,3072]{2,1,0:T(8,128)(2,1)}, bf16[5,5,3,128]{3,2,1,0:T(4,128)(2,1)S(1)}, f32[128]{0:T(128)S(1)}, /*index=5*/s32[]{:T(128)}, f32[]{:T(128)}) while((s32[]{:T(128)}, bf16[4,128,512]{1,2,0:T(8,128)(2,1)}, bf16[4,128,3072]{2,1,0:T(8,128)(2,1)}, ...), condition=%wide.region_2.3_spmd, body=%wide.region_0.2_spmd.sunk | while | flops 1965359104 | bytes 109465424 | solution.py:57
  42.1 19.1 %add_maximum_fusion.2 = f32[128,28,28,128]{3,0,2,1:T(8,128)} fusion(f32[128]{0:T(128)S(1)} %get-tuple-element.169, bf16[128,32,32,3]{0,3,2,1:T(4,128)(2,1)S(1)} %reshape.101, bf16[5,5,3,128]{3,2,1,0:T(4,128)(2,1)S(1)} %get-tuple-element.168), kind=kOutput, calls=%fused_computation.clone.1 | convolution fusion | flops 1952448512 | bytes 52186368 | tf_op jit(solution)/shard_map/while/body/eval_jaxpr/conv_general_dilated | solution.py:34
  61.2 16.1 %reduce_sum.10 = f32[128,2,2,128]{3,0,2,1:T(8,128)S(1)} reduce(f32[128,2,14,2,14,128]{5,0,4,3,2,1:T(8,128)} %bitcast.85, f32[]{:T(128)} %constant.173.clone.1..sunk), dimensions={2,4}, to_apply=%region_1.1 | reduce | flops 12779520 | bytes 51642372 | tf_op jit(solution)/shard_map/while/body/eval_jaxpr/reduce_sum | solution.py:44
  80.1 19.1 %add_maximum_fusion.2 = f32[128,28,28,128]{3,0,2,1:T(8,128)} fusion(f32[128]{0:T(128)S(1)} %get-tuple-element.169, bf16[128,32,32,3]{0,3,2,1:T(4,128)(2,1)S(1)} %reshape.101, bf16[5,5,3,128]{3,2,1,0:T(4,128)(2,1)S(1)} %get-tuple-element.168), kind=kOutput, calls=%fused_computation.clone.1 | convolution fusion | flops 1952448512 | bytes 52186368 | tf_op jit(solution)/shard_map/while/body/eval_jaxpr/conv_general_dilated | solution.py:34
  99.3 16.1 %reduce_sum.10 = f32[128,2,2,128]{3,0,2,1:T(8,128)S(1)} reduce(f32[128,2,14,2,14,128]{5,0,4,3,2,1:T(8,128)} %bitcast.85, f32[]{:T(128)} %constant.173.clone.1..sunk), dimensions={2,4}, to_apply=%region_1.1 | reduce | flops 12779520 | bytes 51642372 | tf_op jit(solution)/shard_map/while/body/eval_jaxpr/reduce_sum | solution.py:44
  118.2 19.1 %add_maximum_fusion.2 = f32[128,28,28,128]{3,0,2,1:T(8,128)} fusion(f32[128]{0:T(128)S(1)} %get-tuple-element.169, bf16[128,32,32,3]{0,3,2,1:T(4,128)(2,1)S(1)} %reshape.101, bf16[5,5,3,128]{3,2,1,0:T(4,128)(2,1)S(1)} %get-tuple-element.168), kind=kOutput, calls=%fused_computation.clone.1 | convolution fusion | flops 1952448512 | bytes 52186368 | tf_op jit(solution)/shard_map/while/body/eval_jaxpr/conv_general_dilated | solution.py:34
  137.3 16.1 %reduce_sum.10 = f32[128,2,2,128]{3,0,2,1:T(8,128)S(1)} reduce(f32[128,2,14,2,14,128]{5,0,4,3,2,1:T(8,128)} %bitcast.85, f32[]{:T(128)} %constant.173.clone.1..sunk), dimensions={2,4}, to_apply=%region_1.1 | reduce | flops 12779520 | bytes 51642372 | tf_op jit(solution)/shard_map/while/body/eval_jaxpr/reduce_sum | solution.py:44
  156.3 19.1 %add_maximum_fusion.2 = f32[128,28,28,128]{3,0,2,1:T(8,128)} fusion(f32[128]{0:T(128)S(1)} %get-tuple-element.169, bf16[128,32,32,3]{0,3,2,1:T(4,128)(2,1)S(1)} %reshape.101, bf16[5,5,3,128]{3,2,1,0:T(4,128)(2,1)S(1)} %get-tuple-element.168), kind=kOutput, calls=%fused_computation.clone.1 | convolution fusion | flops 1952448512 | bytes 52186368 | tf_op jit(solution)/shard_map/while/body/eval_jaxpr/conv_general_dilated | solution.py:34
  175.4 16.1 %reduce_sum.10 = f32[128,2,2,128]{3,0,2,1:T(8,128)S(1)} reduce(f32[128,2,14,2,14,128]{5,0,4,3,2,1:T(8,128)} %bitcast.85, f32[]{:T(128)} %constant.173.clone.1..sunk), dimensions={2,4}, to_apply=%region_1.1 | reduce | flops 12779520 | bytes 51642372 | tf_op jit(solution)/shard_map/while/body/eval_jaxpr/reduce_sum | solution.py:44
  200.3 82.0 %all-reduce.4.cloned.1.call-done = f32[512,512]{1,0:T(8,128)} async-done(((f32[512,512]{1,0:T(8,128)}), f32[512,512]{1,0:T(8,128)}) %all-reduce.4.cloned.1.call-update) | async-done | bytes 1048592 | tf_op jit(solution)/shard_map/psum | solution.py:64
  290.0 11.7 %cholesky.103 = f32[128,128]{1,0:T(8,128)S(1)} custom-call(f32[128,128]{1,0:T(8,128)S(1)} %cholesky.263), custom_call_target="Cholesky" | custom-call | tf_op jit(solution)/shard_map/jit(cholesky)/cholesky | solution.py:70
  302.8 9.8 %custom-call.32 = f32[1,128,128]{1,2,0:T(8,128)S(1)} custom-call(f32[1,128,128]{2,1,0:T(8,128)S(1)} %get-tuple-element.86), custom_call_target="InvertDiagBlocksLowerTriangular" | custom-call | tf_op jit(solution)/shard_map/jit(cholesky)/cholesky | solution.py:70
  315.9 12.1 %cholesky.215 = f32[128,128]{1,0:T(8,128)S(1)} custom-call(f32[128,128]{1,0:T(8,128)S(1)} %cholesky.267), custom_call_target="Cholesky" | custom-call | tf_op jit(solution)/shard_map/jit(cholesky)/cholesky | solution.py:70
  328.6 9.8 %custom-call.33 = f32[1,128,128]{1,2,0:T(8,128)S(1)} custom-call(f32[1,128,128]{2,1,0:T(8,128)S(1)} %get-tuple-element.83), custom_call_target="InvertDiagBlocksLowerTriangular" | custom-call | tf_op jit(solution)/shard_map/jit(cholesky)/cholesky | solution.py:70
  340.8 11.7 %cholesky.236 = f32[128,128]{1,0:T(8,128)S(1)} custom-call(f32[128,128]{1,0:T(8,128)S(1)} %cholesky.272), custom_call_target="Cholesky" | custom-call | tf_op jit(solution)/shard_map/jit(cholesky)/cholesky | solution.py:70
  353.1 9.8 %custom-call.34 = f32[1,128,128]{1,2,0:T(8,128)S(1)} custom-call(f32[1,128,128]{2,1,0:T(8,128)S(1)} %get-tuple-element.80), custom_call_target="InvertDiagBlocksLowerTriangular" | custom-call | tf_op jit(solution)/shard_map/jit(cholesky)/cholesky | solution.py:70
  365.2 11.9 %cholesky.253 = f32[128,128]{1,0:T(8,128)S(1)} custom-call(f32[128,128]{1,0:T(8,128)S(1)} %convolution_subtract_fusion.6), custom_call_target="Cholesky" | custom-call | tf_op jit(solution)/shard_map/jit(cholesky)/cholesky | solution.py:70
  384.4 14.6 %while.12 = (s32[]{:T(128)}, f32[512,512]{1,0:T(8,128)}, s32[4,2]{0,1:T(2,128)S(1)}, f32[4,128,128]{2,1,0:T(8,128)}, s32[]{:T(128)}) while((s32[]{:T(128)}, f32[512,512]{1,0:T(8,128)}, s32[4,2]{0,1:T(2,128)S(1)}, f32[4,128,128]{2,1,0:T(8,128)}, s32[]{:T(128)}) %tuple.52), condition=%wide.while_cond, body=%wide.while_body.sunk | while | flops 2 | bytes 132705 | solution.py:15
  385.1 3.0 bitcast_dynamic-update-slice_fusion.2
  388.7 3.0 bitcast_dynamic-update-slice_fusion.2
  399.0 40.1 %custom-call.35 = f32[4,128,128]{1,2,0:T(8,128)S(1)} custom-call(f32[4,128,128]{2,1,0:T(8,128)} %get-tuple-element.41), custom_call_target="InvertDiagBlocksLowerTriangular" | custom-call | tf_op jit(solution)/shard_map/triangular_solve | solution.py:15
  439.1 28.5 %all-reduce.6.cloned.1.call-done = f32[512,1000]{0,1:T(8,128)} async-done(((f32[512,1000]{0,1:T(8,128)}), f32[512,1000]{0,1:T(8,128)}) %all-reduce.6.cloned.1.call-update) | async-done | bytes 2048016 | tf_op jit(solution)/shard_map/psum | solution.py:67
  488.2 31.7 %reduce-scatter.2.cloned.1.call-done = bf16[64,1000]{1,0:T(8,128)(2,1)} async-done(((bf16[512,1000]{1,0:T(8,128)(2,1)}), bf16[64,1000]{1,0:T(8,128)(2,1)}) %reduce-scatter.2.cloned.1.call-update) | async-done | bytes 128016 | tf_op jit(solution)/shard_map/reduce_scatter | solution.py:73
  (107 shorter events, 77.4 us)
Async XLA Ops:
  7.2 32.9 %all-gather.2.cloned.1.call-start = ((), (), s32[]{:S(2)}) async-start(), calls=%async_computation.1 | async-start | bytes 3538944 | tf_op jit(solution)/shard_map/all_gather | solution.py:53
  7.9 274.4 %all-reduce.4.cloned.1.call-start = ((), (), s32[]{:S(2)}) async-start(), calls=%async_computation.2 | async-start | bytes 2097152 | tf_op jit(solution)/shard_map/psum | solution.py:64
  8.7 31.4 %copy-start.5 = (f32[128]{0:T(128)S(1)}, f32[128]{0:T(128)}, u32[]{:S(2)}) copy-start(f32[128]{0:T(128)} %param.11) | copy-start | bytes 1540
  192.4 3.0 copy-start.4
  195.1 2.1 copy-start.1
  195.1 272.5 %all-reduce.6.cloned.1.call-start = ((), (), s32[]{:S(2)}) async-start(), calls=%async_computation.3 | async-start | bytes 4096000 | tf_op jit(solution)/shard_map/psum | solution.py:67
  289.0 1.0 copy-start.3
  377.1 7.3 %copy-start.6 = (s32[4]{0:T(128)S(1)}, s32[4]{0:T(128)}, u32[]{:S(2)}) copy-start(s32[4]{0:T(128)} %iota_multiply_fusion) | copy-start | bytes 52
  377.1 142.7 %reduce-scatter.2.cloned.1.call-start = ((), (), s32[]{:S(2)}) async-start(), calls=%async_computation.4 | async-start | bytes 1179648 | tf_op jit(solution)/shard_map/reduce_scatter | solution.py:73
  467.6 2.8 copy-start.2
  485.1 1.3 copy-start
Sparse Core Ops, SparseCore 0:
  9.7 30.3 all-gather.1
  195.2 86.9 all-reduce.3
  377.2 90.3 all-reduce.5
  488.3 31.4 reduce-scatter.1
